TPU v7x, 512 devices: a whole 4x8x8 slice. The times are simulated.
512 devices in a mesh: slab: 64 (over z, x, core), obs: 8 (over y).
Axes of the slice: x: 4, y: 8, z: 8, core: 2. Of those that a mesh axis runs over, the one named last changes fastest.
Arguments:
- background_members: float32 [64, 1048576], P('slab', 'obs'), may hold values from -6 to 6
- measurement_jitter: bfloat16 [64, 8, 65536], P(None, 'obs', 'slab'), may hold values from -5 to 5
- measurement_readings: float32 [8, 65536], P('obs', 'slab'), may hold values from -8 to 8
- measurement_noise_spread: float32 [8, 65536], P('obs', 'slab'), may hold values from 0.2 to 2
- measurement_grid_location: int32 [8, 65536], P('obs', 'slab'), may hold values from 0 to 2047
- active_tallies: int32 [8, 64], P('obs', 'slab'), may hold values from 128 to 1024, as said below
- coupling_listing: int32 [8, 2048, 8], P('obs', 'slab'), may hold values from 0 to 63, as said below
- taper_factors: float32 [8, 2048, 8], P('obs', 'slab'), may hold values from 0.1 to 1
Outputs:
- analysis: float32 [64, 1048576], P('slab', 'obs')
Inputs may be any that keep to these rules, and one draw needn't show every extreme that they name: `active_tallies`: some region of some group holds 1024 live observations; slots beyond a region's count are padding. `coupling_listing`: the 8 observation blocks listed for a state block are distinct.
All inputs are finite; a program needn't handle non-finite values.
Results may differ from a plain program's by a relative error of at most 0.0063.
Values may be sent and summed in bfloat16 or wider, within the bound.
No kernel may reach another device: no remote copies, remote signals or barrier semaphores. Data moves between devices by JAX's collectives and lax.ppermute only.
A program may use at most 64 MiB of HBM per device.

v0:
```python
import jax
import jax.numpy as jnp
from jax import lax
from jax.sharding import PartitionSpec as P

OB = 128
highest = lax.Precision.HIGHEST


def block_products(
    tile_work,
    measurement_jitter,
    measurement_readings,
    measurement_noise_spread,
    measurement_grid_location,
    active_tallies,
):
    members = tile_work.shape[0]
    positions = measurement_grid_location[0]
    obs_count = positions.shape[0]
    prior_value = jnp.take(tile_work, positions, axis=1)
    prior_shift = prior_value - jnp.mean(prior_value, axis=0, keepdims=True)
    spread = jnp.sum(prior_shift * prior_shift, axis=0, keepdims=True) / (members - 1)
    usable = jnp.arange(obs_count, dtype=jnp.int32)[None, :] < active_tallies[0, 0]
    innovation = (
        measurement_readings + measurement_jitter[:, 0, :].astype(jnp.float32) - prior_value
    ) / (spread + measurement_noise_spread)
    gain_input = jnp.where(usable, innovation, jnp.float32(0.0)).astype(jnp.bfloat16)
    prior_low = prior_shift.astype(jnp.bfloat16)
    return jnp.einsum(
        "mco,nco->cmn",
        gain_input.reshape(members, -1, OB),
        prior_low.reshape(members, -1, OB),
        preferred_element_type=jnp.float32,
    )


def local(
    background_members,
    measurement_jitter,
    measurement_readings,
    measurement_noise_spread,
    measurement_grid_location,
    active_tallies,
    coupling_listing,
    taper_factors,
):
    work_low = background_members.astype(jnp.bfloat16)
    tile_low = lax.all_to_all(work_low, "slab", split_axis=1, concat_axis=0, tiled=True)
    tile_work = tile_low.astype(jnp.float32)
    members = tile_work.shape[0]
    blocks = coupling_listing.shape[1]
    deviation = tile_work - jnp.mean(tile_work, axis=0, keepdims=True)
    products = block_products(
        tile_work,
        measurement_jitter,
        measurement_readings,
        measurement_noise_spread,
        measurement_grid_location,
        active_tallies,
    )
    all_products = lax.all_gather(products, "obs", axis=0, tiled=True)
    obs_blocks = all_products.shape[0]
    block_links = coupling_listing[0]
    factor = taper_factors[0] / (members - 1)
    choose = block_links[..., None] == jnp.arange(obs_blocks, dtype=jnp.int32)
    localize = jnp.sum(jnp.where(choose, factor[..., None], jnp.float32(0.0)), axis=1)
    ensemble = jnp.einsum("bc,cmn->bmn", localize, all_products, precision=highest)
    region_dev = deviation.reshape(members, blocks, -1)
    increment = jnp.einsum("bmn,nbp->mbp", ensemble, region_dev, precision=highest)
    increment_low = increment.reshape(members, -1).astype(jnp.bfloat16)
    back = lax.all_to_all(increment_low, "slab", split_axis=0, concat_axis=1, tiled=True)
    return background_members + back.astype(jnp.float32)


def solution(mesh):
    return jax.shard_map(
        local,
        mesh=mesh,
        in_specs=(
            P("slab", "obs"),
            P(None, "obs", "slab"),
            P("obs", "slab"),
            P("obs", "slab"),
            P("obs", "slab"),
            P("obs", "slab"),
            P("obs", "slab", None),
            P("obs", "slab", None),
        ),
        out_specs=P("slab", "obs"),
        check_vma=False,
    )
```

profile of v0, /device:TPU:1, one launch (start us, length us, event | category | flops | bytes accessed | tf_op | source)
XLA Modules:
  0.0 124.3 jit_solution(9766494422847316278)
XLA Ops:
  6.5 0.0 copy-start.1
  6.5 0.0 copy-start.2
  6.5 1.4 %convert_element_type.60 = bf16[1,131072]{1,0:T(2,128)(2,1)S(1)} convert(f32[1,131072]{1,0:T(1,128)} %param.8) | non-fusion elementwise | flops 131072 | bytes 786432 | tf_op jit(solution)/shard_map/convert_element_type | solution.py:48
  8.0 0.5 broadcast.91
  8.5 2.1 %reduce.1 = bf16[64,2048]{1,0:T(8,128)(2,1)S(1)} reduce(bf16[64,1,2048]{2,1,0:T(2,128)(2,1)S(1)} %bitcast.46, bf16[]{:T(256)} %broadcast.91), dimensions={1}, to_apply=%bitcast.40.reduce_sub_computation | reduce | bytes 524290
  10.6 0.9 reshape.167
  11.5 14.8 %all-to-all-start = ((bf16[64,2,1024]{2,1,0:T(2,128)(2,1)}), bf16[64,2,1024]{2,1,0:T(2,128)(2,1)S(1)}, u32[]{:S(2)}, u32[]{:S(2)}) async-start(bf16[64,2,1024]{2,1,0:T(2,128)(2,1)} %reshape.167), calls=%async_computation | async-start | bytes 524288 | tf_op jit(solution)/shard_map/all_to_all | solution.py:49
  26.3 0.0 all-gather.2.cloned.1.call-start
  27.0 0.0 copy-done.1
  27.1 0.0 copy-done.2
  27.2 12.2 %all-to-all-done = bf16[64,2,1024]{2,1,0:T(2,128)(2,1)S(1)} async-done(((bf16[64,2,1024]{2,1,0:T(2,128)(2,1)}), bf16[64,2,1024]{2,1,0:T(2,128)(2,1)S(1)}, u32[]{:S(2)}, u32[]{:S(2)}) %all-to-all-start) | async-done | bytes 262176 | tf_op jit(solution)/shard_map/all_to_all | solution.py:49
  39.4 0.2 reshape.168
  39.7 0.5 copy.28
  40.2 0.1 convert_bitcast_fusion
  40.3 0.0 copy-start.3
  40.3 0.0 copy-start.6
  40.3 2.8 %gather_fusion = f32[1024,64]{1,0:T(8,128)S(1)} fusion(f32[64,2048]{0,1:T(8,128)S(1)} %convert_bitcast_fusion, s32[1024]{0:T(1024)S(1)} %broadcast_clamp_fusion), kind=kCustom, calls=%fused_computation | custom fusion | bytes 528384 | tf_op jit(solution)/shard_map/jit(_take)/gather | solution.py:21
  43.1 0.0 copy-start.5
  43.1 0.0 copy-start.4
  43.1 0.4 fusion.5
  43.5 0.5 multiply_reduce_fusion
  44.0 0.2 copy.32
  44.2 0.0 copy-done.3
  44.2 0.0 copy-done.6
  44.2 0.9 fusion.10
  45.2 0.0 all-gather.2.cloned.1.call-update
  45.2 0.0 copy-done.5
  45.2 0.1 copy.30
  45.3 0.0 copy-done.4
  45.3 0.1 copy.29
  45.4 0.1 select_reduce_fusion
  45.5 0.2 convert_reduce_fusion
  45.7 0.1 div.45
  45.8 34.1 %all-gather.2.cloned.1.call-done = f32[64,64,64]{2,1,0:T(8,128)} async-done(((f32[8,64,64]{2,1,0:T(8,128)}), f32[64,64,64]{2,1,0:T(8,128)}) %all-gather.2.cloned.1.call-update) | async-done | bytes 1048592 | tf_op jit(solution)/shard_map/all_gather | solution.py:62
  80.0 3.9 %fusion = f32[32,64,64]{2,0,1:T(8,128)S(1)} fusion(f32[64,64,64]{2,1,0:T(8,128)} %all-gather.2.cloned.1.call-done, f32[32,64]{1,0:T(8,128)S(1)} %select_reduce_fusion), kind=kOutput, calls=%fused_computation.1 | convolution fusion | flops 100663296 | bytes 1581056 | tf_op jit(solution)/shard_map/bc,cmn->bmn/dot_general | solution.py:68
  83.8 2.3 %convolution_convert_fusion = bf16[32,64,64]{2,1,0:T(8,128)(2,1)S(1)} fusion(f32[32,64,64]{2,0,1:T(8,128)S(1)} %fusion, f32[32,64]{1,0:T(8,128)S(1)} %div.45, bf16[64,32,64]{0,2,1:T(8,128)(2,1)S(1)} %bitcast.43), kind=kOutput, calls=%fused_computation.3 | convolution fusion | flops 101056512 | bytes 1056768 | tf_op jit(solution)/shard_map/bmn,nbp->mbp/dot_general | solution.py:70
  86.2 0.0 copy-start
  86.2 1.1 reduce.2
  87.3 0.2 copy.51
  87.5 0.2 reshape.169
  87.7 28.1 %all_to_all.23 = bf16[64,2,1024]{2,1,0:T(2,128)(2,1)S(1)} all-to-all(bf16[64,2,1024]{2,1,0:T(2,128)(2,1)S(1)} %reshape.169), channel_id=1, replica_groups=mesh['slab'=64,'obs'=8] {'slab'}, dimensions={0} | all-to-all | bytes 524288 | tf_op jit(solution)/shard_map/all_to_all | solution.py:72
  115.8 0.2 reshape.170
  116.0 0.0 copy-done
  116.0 1.5 %convert_add_fusion = f32[1,131072]{1,0:T(1,128)} fusion(f32[1,131072]{1,0:T(1,128)S(1)} %copy-done, bf16[1,131072]{1,0:T(2,128)(2,1)S(1)} %bitcast.45), kind=kLoop, calls=%fused_computation.6 | loop fusion | flops 262144 | bytes 1310720 | tf_op jit(solution)/shard_map/add | solution.py:73
  (11 shorter events, 0.1 us)
Async XLA Ops:
  6.5 20.5 %copy-start.1 = (bf16[64,1,1024]{2,0,1:T(8,128)(2,1)S(1)}, bf16[64,1,1024]{2,0,1:T(8,128)(2,1)}, u32[]{:S(2)}) copy-start(bf16[64,1,1024]{2,0,1:T(8,128)(2,1)} %param.9) | copy-start | bytes 393220
  6.5 20.5 %copy-start.2 = (s32[1,1024]{1,0:T(1,128)S(1)}, s32[1,1024]{1,0:T(1,128)}, u32[]{:S(2)}) copy-start(s32[1,1024]{1,0:T(1,128)} %param.12) | copy-start | bytes 12292
  11.5 27.9 %all-to-all-start = ((bf16[64,2,1024]{2,1,0:T(2,128)(2,1)}), bf16[64,2,1024]{2,1,0:T(2,128)(2,1)S(1)}, u32[]{:S(2)}, u32[]{:S(2)}) async-start(bf16[64,2,1024]{2,1,0:T(2,128)(2,1)} %reshape.167), calls=%async_computation | async-start | bytes 524288 | tf_op jit(solution)/shard_map/all_to_all | solution.py:49
  26.3 53.6 %all-gather.2.cloned.1.call-start = ((), (), s32[]{:S(2)}) async-start(), calls=%async_computation.2 | async-start | bytes 2359296 | tf_op jit(solution)/shard_map/all_gather | solution.py:62
  40.3 4.0 %copy-start.3 = (f32[1,1024]{1,0:T(1,128)S(1)}, f32[1,1024]{1,0:T(1,128)}, u32[]{:S(2)}) copy-start(f32[1,1024]{1,0:T(1,128)} %param.11) | copy-start | bytes 12292
  40.3 4.0 %copy-start.6 = (f32[1,1024]{1,0:T(1,128)S(1)}, f32[1,1024]{1,0:T(1,128)}, u32[]{:S(2)}) copy-start(f32[1,1024]{1,0:T(1,128)} %param.10) | copy-start | bytes 12292
  43.1 2.1 %copy-start.5 = (f32[1,32,8]{1,2,0:T(8,128)S(1)}, f32[1,32,8]{1,2,0:T(8,128)}, u32[]{:S(2)}) copy-start(f32[1,32,8]{1,2,0:T(8,128)} %param.15) | copy-start | bytes 3076
  43.1 2.2 %copy-start.4 = (s32[1,32,8]{1,2,0:T(8,128)S(1)}, s32[1,32,8]{1,2,0:T(8,128)}, u32[]{:S(2)}) copy-start(s32[1,32,8]{1,2,0:T(8,128)} %param.14) | copy-start | bytes 3076
  86.2 29.8 %copy-start = (f32[1,131072]{1,0:T(1,128)S(1)}, f32[1,131072]{1,0:T(1,128)}, u32[]{:S(2)}) copy-start(f32[1,131072]{1,0:T(1,128)} %param.8) | copy-start | bytes 1572868
Sparse Core Ops, SparseCore 0:
  45.3 34.6 all-gather.1
where the time goes:
time: 125 us; the launch traced here: 124 us
  waiting for transfers between devices  46.4 us (37%)
  blocking collectives  28.1 us (22%)
  starting transfers between devices  14.9 us (12%)
  between operations  14.3 us (11%)
  other arithmetic  7.54 us (6%)
  matrix products  7.11 us (6%)
  local copies, waits for them, and re-layouts  6.04 us (5%)
    all_gather x1, waiting for transfers between devices, local(): all_products = lax.all_gather(products, 'obs', axis=0, tiled=True)  34.1 us
    all_to_all x1, blocking collectives, local(): lax.all_to_all(increment_low, 'slab', split_axis=0, concat_axis=1, tiled=...  28.1 us
    all_to_all x1, starting transfers between devices, local(): lax.all_to_all(work_low, 'slab', split_axis=1, concat_axis=0, tiled=True)  14.8 us
    all_to_all x1, waiting for transfers between devices, local(): lax.all_to_all(work_low, 'slab', split_axis=1, concat_axis=0, tiled=True)  12.2 us
    dot_general x1, matrix products, local(): jnp.einsum('bc,cmn->bmn', localize, all_products, precision=highest)  3.85 us
    gather x2, local copies, waits for them, and re-layouts, block_products(): prior_value = jnp.take(tile_work, positions, axis=1)  2.99 us
  transfers between devices with their start and end apart: 2, of which 2 were waited for; matrix products, arithmetic and copies ran while one was open for 1% of the time, Pallas kernels for 0%

commit v1 on v0

--- a/solution.py
+++ b/solution.py
@@ -5,6 +5,12 @@
 
 OB = 128
 highest = lax.Precision.HIGHEST
+
+
+def _treat_zones(u, dim_at):
+    u = jnp.moveaxis(u, 0, dim_at)
+    big = u.shape
+    return u.reshape(*big[:dim_at], big[dim_at] * big[dim_at + 1], *big[dim_at + 2 :])
 
 
 def block_products(
@@ -59,7 +65,23 @@
         measurement_grid_location,
         active_tallies,
     )
-    all_products = lax.all_gather(products, "obs", axis=0, tiled=True)
+    num = jax.lax.axis_size("obs")
+    line_up = tuple(((j, (j + 1) % num) for j in range(num)))
+    parts_seen = tuple(((b, i) for i, b in line_up))
+    kept_arr, value_now = ([], [])
+    for i0 in range(num - 1):
+        if i0 % 2 == 0:
+            kept_arr.append(
+                jax.lax.ppermute(kept_arr[-1] if kept_arr else products, "obs", line_up)
+            )
+        else:
+            value_now.append(
+                jax.lax.ppermute(value_now[-1] if value_now else products, "obs", parts_seen)
+            )
+    found_now = jnp.stack([*kept_arr[::-1], products, *value_now], axis=0)
+    known = jax.lax.axis_index("obs") - len(kept_arr)
+    found_now = found_now[(jnp.arange(num) - known) % num]
+    all_products = _treat_zones(found_now, 0)
     obs_blocks = all_products.shape[0]
     block_links = coupling_listing[0]
     factor = taper_factors[0] / (members - 1)

time: 125 us -> 114 us (0.912)
  starting transfers between devices: 14.9 us -> 37.5 us
  waiting for transfers between devices: 46.4 us -> 28.1 us
  between operations: 14.3 us -> 1.03 us
  local copies, waits for them, and re-layouts: 6.04 us -> 14.1 us
  blocking collectives: 28.1 us -> 20.6 us
  matrix products: 7.11 us -> 4.88 us
    all_gather x1 -> x0, waiting for transfers between devices: 34.1 us -> none  [local(): all_products = lax.all_gather(products, 'obs', axis=0, tiled=True)]
    ppermute x0 -> x7, starting transfers between devices: none -> 22.6 us  [the longest x3 13.7 us: local(): jax.lax.ppermute(value_now[-1] if value_now else products, 'obs', parts_s...]
    ppermute x0 -> x7, waiting for transfers between devices: none -> 15.8 us  [the longest x4 15.8 us: local(): jax.lax.ppermute(kept_arr[-1] if kept_arr else products, 'obs', line_up)]
    all_to_all x1, blocking collectives: 28.1 us -> 20.6 us  [local(): lax.all_to_all(increment_low, 'slab', split_axis=0, concat_axis=1, tiled=...]
    unnamed x21 -> x28, local copies, waits for them, and re-layouts: 2.31 us -> 7.38 us
    gather x0 -> x1, local copies, waits for them, and re-layouts: none -> 2.27 us  [local(): found_now = found_now[(jnp.arange(num) - known) % num]]
    dot_general x1, matrix products: 3.85 us -> 2.33 us  [local(): jnp.einsum('bc,cmn->bmn', localize, all_products, precision=highest)]
  transfers between devices with their start and end apart: 2 -> 8, of which waited for: 2 -> 5; matrix products, arithmetic and copies ran while one was open for 1% -> 5% of each run, Pallas kernels for 0% -> 0%
where the time goes in v1:
time: 114 us
  starting transfers between devices  37.5 us (33%)
  waiting for transfers between devices  28.1 us (25%)
  blocking collectives  20.6 us (18%)
  local copies, waits for them, and re-layouts  14.1 us (12%)
  other arithmetic  7.54 us (7%)
  matrix products  4.88 us (4%)
    all_to_all x1, blocking collectives, local(): lax.all_to_all(increment_low, 'slab', split_axis=0, concat_axis=1, tiled=...  20.6 us
    ppermute x4, waiting for transfers between devices, local(): jax.lax.ppermute(kept_arr[-1] if kept_arr else products, 'obs', line_up)  15.8 us
    all_to_all x1, starting transfers between devices, local(): lax.all_to_all(work_low, 'slab', split_axis=1, concat_axis=0, tiled=True)  14.8 us
    ppermute x3, starting transfers between devices, local(): jax.lax.ppermute(value_now[-1] if value_now else products, 'obs', parts_s...  13.7 us
    all_to_all x1, waiting for transfers between devices, local(): lax.all_to_all(work_low, 'slab', split_axis=1, concat_axis=0, tiled=True)  12.3 us
    ppermute x4, starting transfers between devices, local(): jax.lax.ppermute(kept_arr[-1] if kept_arr else products, 'obs', line_up)  8.93 us
    unnamed x28, local copies, waits for them, and re-layouts  7.38 us
    gather x2, local copies, waits for them, and re-layouts, block_products(): prior_value = jnp.take(tile_work, positions, axis=1)  2.99 us
  transfers between devices with their start and end apart: 8, of which 5 were waited for; matrix products, arithmetic and copies ran while one was open for 5% of the time, Pallas kernels for 0%

profile of v1, /device:TPU:1, one launch (start us, length us, event | category | flops | bytes accessed | tf_op | source)
XLA Modules:
  0.0 113.7 jit_solution(716650092378375689)
XLA Ops:
  0.0 0.0 copy-start.1
  0.0 0.0 copy-start.2
  0.0 1.4 %convert_element_type.60 = bf16[1,131072]{1,0:T(2,128)(2,1)S(1)} convert(f32[1,131072]{1,0:T(1,128)} %param.8) | non-fusion elementwise | flops 131072 | bytes 786432 | tf_op jit(solution)/shard_map/convert_element_type | solution.py:54
  1.4 0.5 broadcast.160
  2.0 2.1 %reduce.1 = bf16[64,2048]{1,0:T(8,128)(2,1)S(1)} reduce(bf16[64,1,2048]{2,1,0:T(2,128)(2,1)S(1)} %bitcast.66, bf16[]{:T(256)} %broadcast.160), dimensions={1}, to_apply=%bitcast.59.reduce_sub_computation | reduce | bytes 524290
  4.1 0.9 reshape.228
  5.0 14.8 %all-to-all-start = ((bf16[64,2,1024]{2,1,0:T(2,128)(2,1)}), bf16[64,2,1024]{2,1,0:T(2,128)(2,1)S(1)}, u32[]{:S(2)}, u32[]{:S(2)}) async-start(bf16[64,2,1024]{2,1,0:T(2,128)(2,1)} %reshape.228), calls=%async_computation | async-start | bytes 524288 | tf_op jit(solution)/shard_map/all_to_all | solution.py:55
  20.5 0.0 copy-done.1
  20.5 0.0 copy-done.2
  20.6 12.3 %all-to-all-done = bf16[64,2,1024]{2,1,0:T(2,128)(2,1)S(1)} async-done(((bf16[64,2,1024]{2,1,0:T(2,128)(2,1)}), bf16[64,2,1024]{2,1,0:T(2,128)(2,1)S(1)}, u32[]{:S(2)}, u32[]{:S(2)}) %all-to-all-start) | async-done | bytes 262176 | tf_op jit(solution)/shard_map/all_to_all | solution.py:55
  32.9 0.2 reshape.229
  33.1 0.5 copy.30
  33.7 0.1 convert_bitcast_fusion
  33.7 0.0 copy-start.3
  33.8 0.0 copy-start.6
  33.8 2.8 %gather_fusion = f32[1024,64]{1,0:T(8,128)S(1)} fusion(f32[64,2048]{0,1:T(8,128)S(1)} %convert_bitcast_fusion, s32[1024]{0:T(1024)S(1)} %broadcast_clamp_fusion), kind=kCustom, calls=%fused_computation | custom fusion | bytes 528384 | tf_op jit(solution)/shard_map/jit(_take)/gather | solution.py:27
  36.6 0.0 copy-start.5
  36.6 0.0 copy-start.4
  36.6 0.4 fusion.5
  37.0 0.5 multiply_reduce_fusion
  37.5 0.2 copy.34
  37.7 0.0 copy-done.3
  37.7 0.0 copy-done.6
  37.7 0.2 fusion.10
  37.9 3.2 %collective-permute-start = (f32[8,64,64]{2,1,0:T(8,128)S(1)}, f32[8,64,64]{2,1,0:T(8,128)S(1)}, u32[]{:S(2)}, u32[]{:S(2)}) collective-permute-start(f32[8,64,64]{2,1,0:T(8,128)S(1)} %fusion.10), channel_id=1, source_target_pairs={{0,1},{1,2},{2,3},{3,4},{4,5},{5,6},{6,7},{7,0},{8,9},{9,10},{10,1... | collective-permute-start | bytes 393224 | tf_op jit(solution)/shard_map/ppermute | solution.py:75
  41.1 0.0 copy-done.5
  41.2 8.3 %collective-permute-done = f32[8,64,64]{2,1,0:T(8,128)S(1)} collective-permute-done((f32[8,64,64]{2,1,0:T(8,128)S(1)}, f32[8,64,64]{2,1,0:T(8,128)S(1)}, u32[]{:S(2)}, u32[]{:S(2)}) %collective-permute-start) | collective-permute-done | bytes 131104 | tf_op jit(solution)/shard_map/ppermute | solution.py:75
  49.4 1.9 %collective-permute-start.1 = (f32[8,64,64]{2,1,0:T(8,128)S(1)}, f32[8,64,64]{2,1,0:T(8,128)S(1)}, u32[]{:S(2)}, u32[]{:S(2)}) collective-permute-start(f32[8,64,64]{2,1,0:T(8,128)S(1)} %collective-permute-done), channel_id=1, source_target_pairs={{0,1},{1,2},{2,3},{3,4},{4,5},{5,6},{6,7},{7,0},{8,9},{9,10},{10,1... | collective-permute-start | bytes 393224 | tf_op jit(solution)/shard_map/ppermute | solution.py:75
  51.4 0.1 copy.32
  51.5 0.0 copy-done.4
  51.5 0.1 copy.31
  51.5 0.1 select_reduce_fusion
  51.7 4.6 %collective-permute-start.4 = (f32[8,64,64]{2,1,0:T(8,128)S(1)}, f32[8,64,64]{2,1,0:T(8,128)S(1)}, u32[]{:S(2)}, u32[]{:S(2)}) collective-permute-start(f32[8,64,64]{2,1,0:T(8,128)S(1)} %fusion.10), channel_id=1, source_target_pairs={{1,0},{2,1},{3,2},{4,3},{5,4},{6,5},{7,6},{0,7},{9,8},{10,9},{11,1... | collective-permute-start | bytes 393224 | tf_op jit(solution)/shard_map/ppermute | solution.py:79
  56.3 3.3 %collective-permute-done.1 = f32[8,64,64]{2,1,0:T(8,128)S(1)} collective-permute-done((f32[8,64,64]{2,1,0:T(8,128)S(1)}, f32[8,64,64]{2,1,0:T(8,128)S(1)}, u32[]{:S(2)}, u32[]{:S(2)}) %collective-permute-start.1) | collective-permute-done | bytes 131104 | tf_op jit(solution)/shard_map/ppermute | solution.py:75
  59.6 1.9 %collective-permute-start.2 = (f32[8,64,64]{2,1,0:T(8,128)S(1)}, f32[8,64,64]{2,1,0:T(8,128)S(1)}, u32[]{:S(2)}, u32[]{:S(2)}) collective-permute-start(f32[8,64,64]{2,1,0:T(8,128)S(1)} %collective-permute-done.1), channel_id=1, source_target_pairs={{0,1},{1,2},{2,3},{3,4},{4,5},{5,6},{6,7},{7,0},{8,9},{9,10},{10,1... | collective-permute-start | bytes 393224 | tf_op jit(solution)/shard_map/ppermute | solution.py:75
  61.5 0.2 convert_reduce_fusion
  61.7 0.0 collective-permute-done.4
  61.7 4.6 %collective-permute-start.5 = (f32[8,64,64]{2,1,0:T(8,128)S(1)}, f32[8,64,64]{2,1,0:T(8,128)S(1)}, u32[]{:S(2)}, u32[]{:S(2)}) collective-permute-start(f32[8,64,64]{2,1,0:T(8,128)S(1)} %collective-permute-done.4), channel_id=1, source_target_pairs={{1,0},{2,1},{3,2},{4,3},{5,4},{6,5},{7,6},{0,7},{9,8},{10,9},{11,1... | collective-permute-start | bytes 393224 | tf_op jit(solution)/shard_map/ppermute | solution.py:79
  66.3 2.5 %collective-permute-done.2 = f32[8,64,64]{2,1,0:T(8,128)S(1)} collective-permute-done((f32[8,64,64]{2,1,0:T(8,128)S(1)}, f32[8,64,64]{2,1,0:T(8,128)S(1)}, u32[]{:S(2)}, u32[]{:S(2)}) %collective-permute-start.2) | collective-permute-done | bytes 131104 | tf_op jit(solution)/shard_map/ppermute | solution.py:75
  68.8 1.9 %collective-permute-start.3 = (f32[8,64,64]{2,1,0:T(8,128)S(1)}, f32[8,64,64]{2,1,0:T(8,128)S(1)}, u32[]{:S(2)}, u32[]{:S(2)}) collective-permute-start(f32[8,64,64]{2,1,0:T(8,128)S(1)} %collective-permute-done.2), channel_id=1, source_target_pairs={{0,1},{1,2},{2,3},{3,4},{4,5},{5,6},{6,7},{7,0},{8,9},{9,10},{10,1... | collective-permute-start | bytes 393224 | tf_op jit(solution)/shard_map/ppermute | solution.py:75
  70.7 0.1 div.45
  70.8 0.0 collective-permute-done.5
  70.8 4.6 %collective-permute-start.6 = (f32[8,64,64]{2,1,0:T(8,128)S(1)}, f32[8,64,64]{2,1,0:T(8,128)S(1)}, u32[]{:S(2)}, u32[]{:S(2)}) collective-permute-start(f32[8,64,64]{2,1,0:T(8,128)S(1)} %collective-permute-done.5), channel_id=1, source_target_pairs={{1,0},{2,1},{3,2},{4,3},{5,4},{6,5},{7,6},{0,7},{9,8},{10,9},{11,1... | collective-permute-start | bytes 393224 | tf_op jit(solution)/shard_map/ppermute | solution.py:79
  75.4 1.7 %collective-permute-done.3 = f32[8,64,64]{2,1,0:T(8,128)S(1)} collective-permute-done((f32[8,64,64]{2,1,0:T(8,128)S(1)}, f32[8,64,64]{2,1,0:T(8,128)S(1)}, u32[]{:S(2)}, u32[]{:S(2)}) %collective-permute-start.3) | collective-permute-done | bytes 131104 | tf_op jit(solution)/shard_map/ppermute | solution.py:75
  77.1 0.7 bitcast_dynamic-update-slice_fusion.7
  77.8 0.7 bitcast_dynamic-update-slice_fusion.6
  78.6 0.7 bitcast_dynamic-update-slice_fusion.5
  79.3 0.7 bitcast_dynamic-update-slice_fusion.4
  80.0 0.7 bitcast_dynamic-update-slice_fusion.3
  80.7 0.7 bitcast_dynamic-update-slice_fusion.2
  81.5 0.7 bitcast_dynamic-update-slice_fusion.1
  82.2 0.0 collective-permute-done.6
  82.2 0.7 bitcast_dynamic-update-slice_fusion
  82.9 2.3 %gather_fusion.1 = f32[8,8,64,64]{3,2,1,0:T(8,128)S(1)} fusion(f32[8,8,64,64]{3,2,1,0:T(8,128)} %bitcast_dynamic-update-slice_fusion, s32[1024]{0:T(1024)S(1)} %pad_clamp_fusion), kind=kCustom, calls=%fused_computation.1 | custom fusion | bytes 2097184 | tf_op jit(solution)/shard_map/gather | solution.py:83
  85.2 2.3 %fusion = f32[32,64,64]{2,0,1:T(8,128)S(1)} fusion(f32[64,64,64]{2,1,0:T(8,128)S(1)} %bitcast.62, f32[32,64]{1,0:T(8,128)S(1)} %select_reduce_fusion), kind=kOutput, calls=%fused_computation.2 | convolution fusion | flops 100663296 | bytes 1581056 | tf_op jit(solution)/shard_map/bc,cmn->bmn/dot_general | solution.py:90
  87.5 2.3 %convolution_convert_fusion = bf16[32,64,64]{2,1,0:T(8,128)(2,1)S(1)} fusion(f32[32,64,64]{2,0,1:T(8,128)S(1)} %fusion, f32[32,64]{1,0:T(8,128)S(1)} %div.45, bf16[64,32,64]{0,2,1:T(8,128)(2,1)S(1)} %bitcast.63), kind=kOutput, calls=%fused_computation.4 | convolution fusion | flops 101056512 | bytes 1056768 | tf_op jit(solution)/shard_map/bmn,nbp->mbp/dot_general | solution.py:92
  89.9 0.0 copy-start
  89.9 1.1 reduce.2
  91.0 0.2 copy.53
  91.2 0.2 reshape.230
  91.4 20.6 %all_to_all.23 = bf16[64,2,1024]{2,1,0:T(2,128)(2,1)S(1)} all-to-all(bf16[64,2,1024]{2,1,0:T(2,128)(2,1)S(1)} %reshape.230), channel_id=1, replica_groups=mesh['slab'=64,'obs'=8] {'slab'}, dimensions={0} | all-to-all | bytes 524288 | tf_op jit(solution)/shard_map/all_to_all | solution.py:94
  112.0 0.2 reshape.231
  112.2 0.0 copy-done
  112.2 1.5 %convert_add_fusion = f32[1,131072]{1,0:T(1,128)} fusion(f32[1,131072]{1,0:T(1,128)S(1)} %copy-done, bf16[1,131072]{1,0:T(2,128)(2,1)S(1)} %bitcast.65), kind=kLoop, calls=%fused_computation.7 | loop fusion | flops 262144 | bytes 1310720 | tf_op jit(solution)/shard_map/add | solution.py:95
  (13 shorter events, 0.1 us)
Async XLA Ops:
  0.0 20.5 %copy-start.1 = (bf16[64,1,1024]{2,0,1:T(8,128)(2,1)S(1)}, bf16[64,1,1024]{2,0,1:T(8,128)(2,1)}, u32[]{:S(2)}) copy-start(bf16[64,1,1024]{2,0,1:T(8,128)(2,1)} %param.9) | copy-start | bytes 393220
  0.0 20.5 %copy-start.2 = (s32[1,1024]{1,0:T(1,128)S(1)}, s32[1,1024]{1,0:T(1,128)}, u32[]{:S(2)}) copy-start(s32[1,1024]{1,0:T(1,128)} %param.12) | copy-start | bytes 12292
  5.0 27.9 %all-to-all-start = ((bf16[64,2,1024]{2,1,0:T(2,128)(2,1)}), bf16[64,2,1024]{2,1,0:T(2,128)(2,1)S(1)}, u32[]{:S(2)}, u32[]{:S(2)}) async-start(bf16[64,2,1024]{2,1,0:T(2,128)(2,1)} %reshape.228), calls=%async_computation | async-start | bytes 524288 | tf_op jit(solution)/shard_map/all_to_all | solution.py:55
  33.7 4.0 %copy-start.3 = (f32[1,1024]{1,0:T(1,128)S(1)}, f32[1,1024]{1,0:T(1,128)}, u32[]{:S(2)}) copy-start(f32[1,1024]{1,0:T(1,128)} %param.11) | copy-start | bytes 12292
  33.8 4.0 %copy-start.6 = (f32[1,1024]{1,0:T(1,128)S(1)}, f32[1,1024]{1,0:T(1,128)}, u32[]{:S(2)}) copy-start(f32[1,1024]{1,0:T(1,128)} %param.10) | copy-start | bytes 12292
  36.6 4.6 %copy-start.5 = (f32[1,32,8]{1,2,0:T(8,128)S(1)}, f32[1,32,8]{1,2,0:T(8,128)}, u32[]{:S(2)}) copy-start(f32[1,32,8]{1,2,0:T(8,128)} %param.15) | copy-start | bytes 3076
  36.6 14.9 %copy-start.4 = (s32[1,32,8]{1,2,0:T(8,128)S(1)}, s32[1,32,8]{1,2,0:T(8,128)}, u32[]{:S(2)}) copy-start(s32[1,32,8]{1,2,0:T(8,128)} %param.14) | copy-start | bytes 3076
  37.9 11.5 %collective-permute-start = (f32[8,64,64]{2,1,0:T(8,128)S(1)}, f32[8,64,64]{2,1,0:T(8,128)S(1)}, u32[]{:S(2)}, u32[]{:S(2)}) collective-permute-start(f32[8,64,64]{2,1,0:T(8,128)S(1)} %fusion.10), channel_id=1, source_target_pairs={{0,1},{1,2},{2,3},{3,4},{4,5},{5,6},{6,7},{7,0},{8,9},{9,10},{10,1... | collective-permute-start | bytes 393224 | tf_op jit(solution)/shard_map/ppermute | solution.py:75
  49.4 10.1 %collective-permute-start.1 = (f32[8,64,64]{2,1,0:T(8,128)S(1)}, f32[8,64,64]{2,1,0:T(8,128)S(1)}, u32[]{:S(2)}, u32[]{:S(2)}) collective-permute-start(f32[8,64,64]{2,1,0:T(8,128)S(1)} %collective-permute-done), channel_id=1, source_target_pairs={{0,1},{1,2},{2,3},{3,4},{4,5},{5,6},{6,7},{7,0},{8,9},{9,10},{10,1... | collective-permute-start | bytes 393224 | tf_op jit(solution)/shard_map/ppermute | solution.py:75
  51.7 10.0 %collective-permute-start.4 = (f32[8,64,64]{2,1,0:T(8,128)S(1)}, f32[8,64,64]{2,1,0:T(8,128)S(1)}, u32[]{:S(2)}, u32[]{:S(2)}) collective-permute-start(f32[8,64,64]{2,1,0:T(8,128)S(1)} %fusion.10), channel_id=1, source_target_pairs={{1,0},{2,1},{3,2},{4,3},{5,4},{6,5},{7,6},{0,7},{9,8},{10,9},{11,1... | collective-permute-start | bytes 393224 | tf_op jit(solution)/shard_map/ppermute | solution.py:79
  59.6 9.3 %collective-permute-start.2 = (f32[8,64,64]{2,1,0:T(8,128)S(1)}, f32[8,64,64]{2,1,0:T(8,128)S(1)}, u32[]{:S(2)}, u32[]{:S(2)}) collective-permute-start(f32[8,64,64]{2,1,0:T(8,128)S(1)} %collective-permute-done.1), channel_id=1, source_target_pairs={{0,1},{1,2},{2,3},{3,4},{4,5},{5,6},{6,7},{7,0},{8,9},{9,10},{10,1... | collective-permute-start | bytes 393224 | tf_op jit(solution)/shard_map/ppermute | solution.py:75
  61.7 9.1 %collective-permute-start.5 = (f32[8,64,64]{2,1,0:T(8,128)S(1)}, f32[8,64,64]{2,1,0:T(8,128)S(1)}, u32[]{:S(2)}, u32[]{:S(2)}) collective-permute-start(f32[8,64,64]{2,1,0:T(8,128)S(1)} %collective-permute-done.4), channel_id=1, source_target_pairs={{1,0},{2,1},{3,2},{4,3},{5,4},{6,5},{7,6},{0,7},{9,8},{10,9},{11,1... | collective-permute-start | bytes 393224 | tf_op jit(solution)/shard_map/ppermute | solution.py:79
  68.8 8.3 %collective-permute-start.3 = (f32[8,64,64]{2,1,0:T(8,128)S(1)}, f32[8,64,64]{2,1,0:T(8,128)S(1)}, u32[]{:S(2)}, u32[]{:S(2)}) collective-permute-start(f32[8,64,64]{2,1,0:T(8,128)S(1)} %collective-permute-done.2), channel_id=1, source_target_pairs={{0,1},{1,2},{2,3},{3,4},{4,5},{5,6},{6,7},{7,0},{8,9},{9,10},{10,1... | collective-permute-start | bytes 393224 | tf_op jit(solution)/shard_map/ppermute | solution.py:75
  70.8 11.4 %collective-permute-start.6 = (f32[8,64,64]{2,1,0:T(8,128)S(1)}, f32[8,64,64]{2,1,0:T(8,128)S(1)}, u32[]{:S(2)}, u32[]{:S(2)}) collective-permute-start(f32[8,64,64]{2,1,0:T(8,128)S(1)} %collective-permute-done.5), channel_id=1, source_target_pairs={{1,0},{2,1},{3,2},{4,3},{5,4},{6,5},{7,6},{0,7},{9,8},{10,9},{11,1... | collective-permute-start | bytes 393224 | tf_op jit(solution)/shard_map/ppermute | solution.py:79
  89.9 22.3 %copy-start = (f32[1,131072]{1,0:T(1,128)S(1)}, f32[1,131072]{1,0:T(1,128)}, u32[]{:S(2)}) copy-start(f32[1,131072]{1,0:T(1,128)} %param.8) | copy-start | bytes 1572868
